TPU v7x, 256 devices: a whole 4x4x8 slice. The times are simulated.
256 devices in a mesh: fsdp: 16 (over z, core), batch: 16 (over y, x).
Axes of the slice: x: 4, y: 4, z: 8, core: 2. Of those that a mesh axis runs over, the one named last changes fastest.
Arguments:
- latents: bfloat16 [16, 16, 1024, 640], P('batch', 'fsdp'), may hold values from -6 to 6
- norm_gain: float32 [640], replicated, may hold values from 0.25 to 1.75
- second_gain: float32 [640], replicated, may hold values from 0.25 to 1.75
- spatial_w: bfloat16 [9, 640, 640], P(None, None, 'fsdp'), may hold values from -0.078125 to 0.078125
- temporal_w: bfloat16 [3, 640, 640], P(None, None, 'fsdp'), may hold values from -0.125 to 0.125
- critic_w: bfloat16 [16, 640, 640], P('batch'), may hold values from -0.25 to 0.25
- critic_head: float32 [16, 640], P('batch'), may hold values from -6 to 6
- targets: int32 [16, 32, 1], P('batch'), may hold values from 0 to 15; in each aligned block of 32 rows (0 to 31, 32 to 63, ..., all dimensions but the last counted through in order) at most 4 rows name the same one
- feasible: int32 [16, 16], P('batch', 'fsdp'), may hold values 0 or 1
Outputs:
- guided: bfloat16 [16, 16, 1024, 640], P('batch', 'fsdp')
Inputs may be any that keep to these rules, and one draw needn't show every extreme that they name: `targets`: among one candidate's 32 rows no critic group is named more than 4 times.
All inputs are finite; a program needn't handle non-finite values. No bound on the sum of `feasible` on one device may be relied on, other than what follows from the above.
Results may differ from a plain program's by a relative error of at most 0.0065.
Values may be sent and summed in bfloat16 or wider, within the bound.
No kernel may reach another device: no remote copies, remote signals or barrier semaphores. Data moves between devices by JAX's collectives and lax.ppermute only.
A program may use at most 128 MiB of HBM per device.

v0:
```python
import jax
import jax.numpy as jnp
import numpy as np
from jax import lax
from jax.sharding import Mesh
from jax.sharding import PartitionSpec as P

GROUPS = 32
IMG_ROWS = 32
IMG_COLS = 32
PIX = 1024
CAP = 4
FSDP = ("z", "c")
BATCH = ("y", "x")


def with_halo(array, axis, dim):
    size, length = (lax.axis_size(axis), array.shape[dim])
    up = [(i, (i + 1) % size) for i in range(size - 1)]
    down = [(j, i) for i, j in up]
    last = lax.slice_in_dim(array, length - 1, length, axis=dim)
    leading = lax.slice_in_dim(array, 0, 1, axis=dim)
    before = lax.ppermute(last, axis, up)
    after = lax.ppermute(leading, axis, down)
    return jnp.concatenate([before, array, after], axis=dim)


def group_silu(values, gain):
    shape = values.shape
    width = shape[-1]
    grouped = values.astype(jnp.float32).reshape(-1, shape[-2], GROUPS, width // GROUPS)
    center = jnp.mean(grouped, axis=(1, 3), keepdims=True)
    spread = jnp.mean((grouped - center) ** 2, axis=(1, 3), keepdims=True)
    normed = ((grouped - center) * lax.rsqrt(spread + 1e-05)).reshape(shape) * gain
    return jax.nn.silu(normed).astype(jnp.bfloat16)


def gather_out_major(weights):
    turned = jnp.swapaxes(weights, 1, 2)
    return lax.all_gather(turned, FSDP, axis=1, tiled=True)


def nt_dot(a, b):
    return lax.dot_general(a, b, (((1,), (1,)), ((), ())), preferred_element_type=jnp.float32)


def per_device(
    latents, norm_gain, second_gain, spatial_w, temporal_w, critic_w, critic_head, targets, feasible
):
    cands = latents.shape[0]
    width = latents.shape[-1]
    hid = critic_w.shape[-1]
    core = lax.axis_index("c")
    half = hid // 2
    own_half = lax.dynamic_slice_in_dim(critic_w[0], core * half, half, axis=1)
    mine = lax.all_gather(own_half, BATCH, axis=0, tiled=False)
    other = lax.ppermute(mine, "c", [(0, 1), (1, 0)])
    heads = lax.all_gather(critic_head[0], BATCH, axis=0, tiled=False)
    heads_mine = lax.dynamic_slice_in_dim(heads, core * half, half, axis=1)
    heads_other = lax.dynamic_slice_in_dim(heads, (1 - core) * half, half, axis=1)
    spatial_full = gather_out_major(spatial_w)
    temporal_full = gather_out_major(temporal_w)
    first = group_silu(latents, norm_gain)
    padded = jnp.pad(
        first.reshape(cands, IMG_ROWS, IMG_COLS, width), ((0, 0), (1, 1), (1, 1), (0, 0))
    )
    total = jnp.zeros((cands * PIX, spatial_full.shape[1]), jnp.float32)
    for offset in range(9):
        row_off, col_off = divmod(offset, 3)
        window = padded[:, row_off : row_off + IMG_ROWS, col_off : col_off + IMG_COLS].reshape(
            -1, width
        )
        total = total + nt_dot(window, spatial_full[offset])
    section = (latents.astype(jnp.float32) + total.reshape(latents.shape)).astype(jnp.bfloat16)
    second = group_silu(section, second_gain)
    beside_all = with_halo(second, FSDP, 1)
    total = jnp.zeros((cands * PIX, temporal_full.shape[1]), jnp.float32)
    for tap in range(3):
        total = total + nt_dot(beside_all[:, tap].reshape(-1, width), temporal_full[tap])
    denoised = (section.astype(jnp.float32) + total.reshape(latents.shape)).astype(jnp.bfloat16)
    groups = mine.shape[0]
    slots = cands * CAP
    flat_targets = targets.reshape(-1)
    chosen = (flat_targets[:, None] == jnp.arange(groups, dtype=jnp.int32)[None, :]).astype(
        jnp.int32
    )
    earlier = jnp.cumsum(chosen, axis=0) - chosen
    slot_of = jnp.sum(earlier * chosen, axis=1)
    live = jnp.repeat(feasible.reshape(-1), IMG_ROWS) > 0
    position = flat_targets * slots + slot_of
    placing = (
        (jnp.arange(groups * slots, dtype=jnp.int32)[:, None] == position[None, :]) & live[None, :]
    ).astype(jnp.bfloat16)
    rows = denoised.reshape(cands * IMG_ROWS, IMG_COLS * width)
    block = (
        jnp.dot(placing, rows, preferred_element_type=jnp.float32)
        .astype(jnp.bfloat16)
        .reshape(groups, slots * IMG_COLS, width)
    )

    def slope_of(w, h):
        pre = jnp.einsum("gtc,gch->gth", block, w, preferred_element_type=jnp.float32)
        return ((1.0 - jnp.tanh(pre) ** 2) * h[:, None, :]).astype(jnp.bfloat16)

    grads = jnp.einsum(
        "gth,gch->gtc", slope_of(mine, heads_mine), mine, preferred_element_type=jnp.float32
    ) + jnp.einsum(
        "gth,gch->gtc", slope_of(other, heads_other), other, preferred_element_type=jnp.float32
    )
    returned = grads.astype(jnp.bfloat16).reshape(groups * slots, -1)
    back = jnp.dot(placing.T, returned, preferred_element_type=jnp.float32)
    guided = (rows.astype(jnp.float32) - back).astype(jnp.bfloat16)
    return guided.reshape(latents.shape)


def solution(mesh):
    fine = Mesh(np.asarray(mesh.devices).reshape(8, 2, 4, 4), ("z", "c", "y", "x"))
    in_specs = (
        P(BATCH, FSDP, None, None),
        P(),
        P(),
        P(None, None, FSDP),
        P(None, None, FSDP),
        P(BATCH, None, None),
        P(BATCH, None),
        P(BATCH, None, None),
        P(BATCH, FSDP),
    )
    out_specs = P(BATCH, FSDP, None, None)
    return jax.shard_map(
        per_device, mesh=fine, in_specs=in_specs, out_specs=out_specs, check_vma=False
    )
```

profile of v0, /device:TPU:1, one launch (start us, length us, event | category | flops | bytes accessed | tf_op | source)
XLA Modules:
  0.0 253.1 jit_solution(7458203786415808206)
XLA Ops:
  6.5 1.1 copy-done
  7.9 1.0 copy.15
  11.9 0.8 fusion.20
  12.7 5.3 %pad_slice_fusion = (bf16[1,32,32,640]{3,2,1,0:T(8,128)(2,1)}, bf16[1,32,32,640]{3,2,1,0:T(8,128)(2,1)}, bf16[1,32,32,640]{3,2,1,0:T(8,128)(2,1)}, bf16[1,32,32,...) fusion(bf16[1,32,32,640]{3,2,1,0:T(8,128)(2,1)S(1)} %bitcast.93), kind=kLoop, calls=%fused_computation.34 | loop fusion | bytes 11796480 | tf_op jit(solution)/shard_map/slice | solution.py:70
  18.0 62.9 %all-gather.9.cloned.1.call-done = bf16[16,640,320]{1,2,0:T(8,128)(2,1)} async-done(((bf16[1,640,320]{1,2,0:T(8,128)(2,1)}), bf16[16,640,320]{1,2,0:T(8,128)(2,1)}) %all-gather.9.cloned.1.call-update) | async-done | bytes 6553616 | tf_op jit(solution)/shard_map/all_gather | solution.py:56
  80.9 0.8 collective-permute-start.2
  81.8 52.3 %all-gather.5.cloned.1.call-done = bf16[9,640,640]{2,1,0:T(8,128)(2,1)} async-done(((bf16[9,40,640]{2,1,0:T(8,128)(2,1)}), bf16[9,640,640]{2,1,0:T(8,128)(2,1)}) %all-gather.5.cloned.1.call-update) | async-done | bytes 7372816 | tf_op jit(solution)/shard_map/all_gather | solution.py:40
  134.1 2.6 %fusion.32 = f32[1024,640]{1,0:T(8,128)S(1)} fusion(bf16[1,1,1024,640]{3,2,1,0:T(8,128)(2,1)S(1)} %fusion.20, bf16[9,640,640]{2,1,0:T(8,128)(2,1)} %all-gather.5.cloned.1.call-done), kind=kOutput, calls=%fused_computation.49 | convolution fusion | flops 838860800 | bytes 4751360 | tf_op jit(solution)/shard_map/dot_general | solution.py:44
  136.7 2.6 %fusion.36 = f32[1024,640]{1,0:T(8,128)S(1)} fusion(bf16[1024,640]{1,0:T(8,128)(2,1)S(1)} %bitcast.101, bf16[9,640,640]{2,1,0:T(8,128)(2,1)} %all-gather.5.cloned.1.call-done), kind=kOutput, calls=%fused_computation.58 | convolution fusion | flops 838860800 | bytes 4751360 | tf_op jit(solution)/shard_map/dot_general | solution.py:44
  139.3 2.6 %fusion.37 = f32[1024,640]{1,0:T(8,128)S(1)} fusion(bf16[1024,640]{1,0:T(8,128)(2,1)S(1)} %bitcast.100, bf16[9,640,640]{2,1,0:T(8,128)(2,1)} %all-gather.5.cloned.1.call-done), kind=kOutput, calls=%fused_computation.60 | convolution fusion | flops 838860800 | bytes 4751360 | tf_op jit(solution)/shard_map/dot_general | solution.py:44
  141.9 2.6 %fusion.38 = f32[1024,640]{1,0:T(8,128)S(1)} fusion(bf16[1024,640]{1,0:T(8,128)(2,1)S(1)} %bitcast.99, bf16[9,640,640]{2,1,0:T(8,128)(2,1)} %all-gather.5.cloned.1.call-done), kind=kOutput, calls=%fused_computation.62 | convolution fusion | flops 838860800 | bytes 4751360 | tf_op jit(solution)/shard_map/dot_general | solution.py:44
  144.5 2.7 %fusion.39 = f32[1024,640]{1,0:T(8,128)S(1)} fusion(bf16[1024,640]{1,0:T(8,128)(2,1)S(1)} %bitcast.98, bf16[9,640,640]{2,1,0:T(8,128)(2,1)} %all-gather.5.cloned.1.call-done), kind=kOutput, calls=%fused_computation.65 | convolution fusion | flops 838860800 | bytes 4751360 | tf_op jit(solution)/shard_map/dot_general | solution.py:44
  147.2 2.6 %fusion.40 = f32[1024,640]{1,0:T(8,128)S(1)} fusion(bf16[1024,640]{1,0:T(8,128)(2,1)S(1)} %bitcast.97, bf16[9,640,640]{2,1,0:T(8,128)(2,1)} %all-gather.5.cloned.1.call-done), kind=kOutput, calls=%fused_computation.67 | convolution fusion | flops 838860800 | bytes 4751360 | tf_op jit(solution)/shard_map/dot_general | solution.py:44
  149.8 2.6 %fusion.41 = f32[1024,640]{1,0:T(8,128)S(1)} fusion(bf16[1024,640]{1,0:T(8,128)(2,1)S(1)} %bitcast.96, bf16[9,640,640]{2,1,0:T(8,128)(2,1)} %all-gather.5.cloned.1.call-done), kind=kOutput, calls=%fused_computation.69 | convolution fusion | flops 838860800 | bytes 4751360 | tf_op jit(solution)/shard_map/dot_general | solution.py:44
  152.4 4.1 %fusion.42 = f32[1024,640]{1,0:T(8,128)} fusion(bf16[1024,640]{1,0:T(8,128)(2,1)S(1)} %bitcast.95, bf16[9,640,640]{2,1,0:T(8,128)(2,1)} %all-gather.5.cloned.1.call-done), kind=kOutput, calls=%fused_computation.71 | convolution fusion | flops 838860800 | bytes 4751360 | tf_op jit(solution)/shard_map/dot_general | solution.py:44
  156.5 3.8 %convert_reduce_fusion = (f32[640]{0:T(1024)S(1)}, bf16[1,1,1024,640]{3,2,1,0:T(8,128)(2,1)S(1)}) fusion(bf16[1024,640]{1,0:T(8,128)(2,1)S(1)} %bitcast.94, bf16[9,640,640]{2,1,0:T(8,128)(2,1)} %all-gather.5.cloned.1.call-done, f32[1024,640]{1,0:T(8,128)S(1)} %fusion.36, f32[1024,640]{1,0:T(8,128)S(1)} %fusion.37, f32[1024,640]{1,0:T(8,128)S(1)} %fusion.38, ...), kind=kOutput, calls=%fused_computation.6 | convolution fusion | flops 847379840 | bytes 25725440 | tf_op jit(solution)/shard_map/dot_general | solution.py:44
  161.5 1.1 fusion.12
  162.6 1.9 collective-permute-start
  165.3 18.4 %all-gather = f32[16,1,640]{2,1,0:T(1,128)S(1)} all-gather(f32[1,1,640]{2,1,0:T(1,128)S(1)} %bitcast.104), channel_id=1, replica_groups=mesh['z'=8,'c'=2,'y'=4,'x'=4] {'y','x'}, dimensions={0}, use_global_device_ids=true | all-gather | bytes 43520 | tf_op jit(solution)/shard_map/all_gather | solution.py:58
  183.7 8.5 %collective-permute-start.1 = (bf16[1,1,1024,640]{3,2,1,0:T(8,128)(2,1)S(1)}, bf16[1,1,1024,640]{3,2,1,0:T(8,128)(2,1)}, u32[]{:S(2)}, u32[]{:S(2)}) collective-permute-start(bf16[1,1,1024,640]{3,2,1,0:T(8,128)(2,1)S(1)} %fusion.12), channel_id=1, source_target_pairs={{16,0},{32,16},{48,32},{64,48},{80,64},{96,80},{112,96},{128,112},... | collective-permute-start | bytes 3932168 | tf_op jit(solution)/shard_map/ppermute | solution.py:24
  192.7 2.6 %fusion.28 = f32[1024,640]{1,0:T(8,128)S(1)} fusion(bf16[1,1,1024,640]{3,2,1,0:T(8,128)(2,1)S(1)} %fusion.12, bf16[3,640,640]{2,1,0:T(8,128)(2,1)} %all-gather.7.cloned.1.call-done), kind=kOutput, calls=%fused_computation.45 | convolution fusion | flops 838860800 | bytes 4751360 | tf_op jit(solution)/shard_map/dot_general | solution.py:44
  195.3 2.7 %fusion.30 = f32[1024,640]{1,0:T(8,128)S(1)} fusion(bf16[1,1,1024,640]{3,2,1,0:T(8,128)(2,1)} %collective-permute-done, bf16[3,640,640]{2,1,0:T(8,128)(2,1)S(1)} %copy-done.13), kind=kOutput, calls=%fused_computation.47 | convolution fusion | flops 838860800 | bytes 4751360 | tf_op jit(solution)/shard_map/dot_general | solution.py:44
  198.0 8.1 %collective-permute-done.1 = bf16[1,1,1024,640]{3,2,1,0:T(8,128)(2,1)} collective-permute-done((bf16[1,1,1024,640]{3,2,1,0:T(8,128)(2,1)S(1)}, bf16[1,1,1024,640]{3,2,1,0:T(8,128)(2,1)}, u32[]{:S(2)}, u32[]{:S(2)}) %collective-permute-start.1) | collective-permute-done | bytes 1310752 | tf_op jit(solution)/shard_map/ppermute | solution.py:24
  206.1 2.8 %fusion.22 = bf16[1,1,1024,640]{3,2,1,0:T(8,128)(2,1)S(1)} fusion(bf16[1,1,1024,640]{3,2,1,0:T(8,128)(2,1)S(1)} %get-tuple-element.16, f32[1024,640]{1,0:T(8,128)S(1)} %fusion.30, f32[1024,640]{1,0:T(8,128)S(1)} %fusion.28, bf16[1,1,1024,640]{3,2,1,0:T(8,128)(2,1)} %collective-permute-done.1, bf16[3,640,640]{2,1,0:T(8,128)(2,1)S(1)} %copy-done.13), kind=kOutput, calls=%fused_computation.31 | convolution fusion | flops 842137600 | bytes 9994240 | tf_op jit(solution)/shard_map/dot_general | solution.py:44
  209.6 1.0 copy-done.3
  210.7 2.3 convolution_convert_fusion
  213.0 3.1 %reshape.219 = bf16[16,128,640]{2,1,0:T(8,128)(2,1)S(1)} reshape(bf16[64,20480]{1,0:T(8,128)(2,1)} %convolution_convert_fusion) | data formatting | bytes 5242880 | tf_op jit(solution)/shard_map/reshape | solution.py:98
  216.2 10.6 %fusion.23 = f32[16,128,640]{2,1,0:T(8,128)} fusion(bf16[16,640,320]{1,2,0:T(8,128)(2,1)} %all-gather.9.cloned.1.call-done, bf16[16,128,640]{2,1,0:T(8,128)(2,1)S(1)} %reshape.219, f32[16,320]{1,0:T(8,128)S(1)} %get-tuple-element.18), kind=kOutput, calls=%fused_computation.42 | convolution fusion | flops 1680343040 | bytes 14438400 | tf_op jit(solution)/shard_map/gth,gch->gtc/dot_general | solution.py:105
  226.8 11.3 %add_convert_fusion = bf16[16,128,640]{2,1,0:T(8,128)(2,1)} fusion(f32[16,128,640]{2,1,0:T(8,128)} %fusion.23, bf16[16,640,320]{1,2,0:T(8,128)(2,1)} %collective-permute-done.2, bf16[16,128,640]{2,1,0:T(8,128)(2,1)S(1)} %reshape.219, f32[16,320]{1,0:T(8,128)S(1)} %get-tuple-element.17), kind=kOutput, calls=%fused_computation.3 | convolution fusion | flops 1682964480 | bytes 17059840 | tf_op jit(solution)/shard_map/gth,gch->gtc/dot_general | solution.py:107
  238.1 4.6 %reshape.220 = bf16[64,20480]{1,0:T(8,128)(2,1)} reshape(bf16[16,128,640]{2,1,0:T(8,128)(2,1)} %add_convert_fusion) | data formatting | bytes 5242880 | tf_op jit(solution)/shard_map/reshape | solution.py:110
  242.7 2.4 fusion
  245.1 1.5 reshape.221
  (74 shorter events, 5.6 us)
Async XLA Ops:
  6.5 1.1 copy-start
  6.5 3.9 %copy-start.2 = (bf16[1,1,1024,640]{3,2,1,0:T(8,128)(2,1)S(1)}, bf16[1,1,1024,640]{3,2,1,0:T(8,128)(2,1)}, u32[]{:S(2)}) copy-start(bf16[1,1,1024,640]{3,2,1,0:T(8,128)(2,1)} %param.9) | copy-start | bytes 3932164
  6.5 74.4 %all-gather.9.cloned.1.call-start = ((), (), s32[]{:S(2)}) async-start(), calls=%async_computation.2 | async-start | bytes 6963200 | tf_op jit(solution)/shard_map/all_gather | solution.py:56
  7.7 4.2 %copy-start.14 = (f32[640]{0:T(1024)S(1)}, f32[640]{0:T(1024)}, u32[]{:S(2)}) copy-start(f32[640]{0:T(1024)} %param.10) | copy-start | bytes 7684
  8.9 125.2 %all-gather.5.cloned.1.call-start = ((), (), s32[]{:S(2)}) async-start(), calls=%async_computation | async-start | bytes 7833600 | tf_op jit(solution)/shard_map/all_gather | solution.py:40
  9.7 183.0 %all-gather.7.cloned.1.call-start = ((), (), s32[]{:S(2)}) async-start(), calls=%async_computation.1 | async-start | bytes 2611200 | tf_op jit(solution)/shard_map/all_gather | solution.py:40
  80.9 145.8 %collective-permute-start.2 = (bf16[16,640,320]{1,2,0:T(8,128)(2,1)}, bf16[16,640,320]{1,2,0:T(8,128)(2,1)}, u32[]{:S(2)}, u32[]{:S(2)}) collective-permute-start(bf16[16,640,320]{1,2,0:T(8,128)(2,1)} %all-gather.9.cloned.1.call-done), channel_id=1, source_target_pairs={{0,16},{16,0},{1,17},{17,1},{2,18},{18,2},{3,19},{19,3},{4,20},{20... | collective-permute-start | bytes 19660808 | tf_op jit(solution)/shard_map/ppermute | solution.py:57
  134.1 2.6 %copy-start.12 = (bf16[1,32,32,640]{3,2,1,0:T(8,128)(2,1)S(1)}, bf16[1,32,32,640]{3,2,1,0:T(8,128)(2,1)}, u32[]{:S(2)}) copy-start(bf16[1,32,32,640]{3,2,1,0:T(8,128)(2,1)} %get-tuple-element.11) | copy-start | bytes 3932164
  136.7 2.6 %copy-start.11 = (bf16[1,32,32,640]{3,2,1,0:T(8,128)(2,1)S(1)}, bf16[1,32,32,640]{3,2,1,0:T(8,128)(2,1)}, u32[]{:S(2)}) copy-start(bf16[1,32,32,640]{3,2,1,0:T(8,128)(2,1)} %get-tuple-element.10) | copy-start | bytes 3932164
  139.3 2.6 %copy-start.10 = (bf16[1,32,32,640]{3,2,1,0:T(8,128)(2,1)S(1)}, bf16[1,32,32,640]{3,2,1,0:T(8,128)(2,1)}, u32[]{:S(2)}) copy-start(bf16[1,32,32,640]{3,2,1,0:T(8,128)(2,1)} %get-tuple-element.9) | copy-start | bytes 3932164
  141.9 2.6 %copy-start.9 = (bf16[1,32,32,640]{3,2,1,0:T(8,128)(2,1)S(1)}, bf16[1,32,32,640]{3,2,1,0:T(8,128)(2,1)}, u32[]{:S(2)}) copy-start(bf16[1,32,32,640]{3,2,1,0:T(8,128)(2,1)} %get-tuple-element.8) | copy-start | bytes 3932164
  144.5 2.7 %copy-start.8 = (bf16[1,32,32,640]{3,2,1,0:T(8,128)(2,1)S(1)}, bf16[1,32,32,640]{3,2,1,0:T(8,128)(2,1)}, u32[]{:S(2)}) copy-start(bf16[1,32,32,640]{3,2,1,0:T(8,128)(2,1)} %get-tuple-element.7) | copy-start | bytes 3932164
  147.2 2.6 %copy-start.7 = (bf16[1,32,32,640]{3,2,1,0:T(8,128)(2,1)S(1)}, bf16[1,32,32,640]{3,2,1,0:T(8,128)(2,1)}, u32[]{:S(2)}) copy-start(bf16[1,32,32,640]{3,2,1,0:T(8,128)(2,1)} %get-tuple-element.6) | copy-start | bytes 3932164
  149.8 2.6 %copy-start.6 = (bf16[1,32,32,640]{3,2,1,0:T(8,128)(2,1)S(1)}, bf16[1,32,32,640]{3,2,1,0:T(8,128)(2,1)}, u32[]{:S(2)}) copy-start(bf16[1,32,32,640]{3,2,1,0:T(8,128)(2,1)} %get-tuple-element.12) | copy-start | bytes 3932164
  152.4 4.1 %copy-start.5 = (bf16[1,32,32,640]{3,2,1,0:T(8,128)(2,1)S(1)}, bf16[1,32,32,640]{3,2,1,0:T(8,128)(2,1)}, u32[]{:S(2)}) copy-start(bf16[1,32,32,640]{3,2,1,0:T(8,128)(2,1)} %get-tuple-element.5) | copy-start | bytes 3932164
  156.5 5.0 %copy-start.15 = (f32[640]{0:T(1024)S(1)}, f32[640]{0:T(1024)}, u32[]{:S(2)}) copy-start(f32[640]{0:T(1024)} %param.11) | copy-start | bytes 7684
  160.3 4.3 %copy-start.17 = (s32[1,32,1]{1,2,0:T(1,128)S(1)}, s32[1,32,1]{1,2,0:T(1,128)}, u32[]{:S(2)}) copy-start(s32[1,32,1]{1,2,0:T(1,128)} %param.16) | copy-start | bytes 388
  160.3 5.0 %copy-start.16 = (f32[1,640]{1,0:T(1,128)S(1)}, f32[1,640]{1,0:T(1,128)}, u32[]{:S(2)}) copy-start(f32[1,640]{1,0:T(1,128)} %param.15) | copy-start | bytes 7684
  162.6 32.7 %collective-permute-start = (bf16[1,1,1024,640]{3,2,1,0:T(8,128)(2,1)S(1)}, bf16[1,1,1024,640]{3,2,1,0:T(8,128)(2,1)}, u32[]{:S(2)}, u32[]{:S(2)}) collective-permute-start(bf16[1,1,1024,640]{3,2,1,0:T(8,128)(2,1)S(1)} %fusion.12), channel_id=1, source_target_pairs={{0,16},{16,32},{32,48},{48,64},{64,80},{80,96},{96,112},{112,128},... | collective-permute-start | bytes 3932168 | tf_op jit(solution)/shard_map/ppermute | solution.py:23
  183.7 22.4 %collective-permute-start.1 = (bf16[1,1,1024,640]{3,2,1,0:T(8,128)(2,1)S(1)}, bf16[1,1,1024,640]{3,2,1,0:T(8,128)(2,1)}, u32[]{:S(2)}, u32[]{:S(2)}) collective-permute-start(bf16[1,1,1024,640]{3,2,1,0:T(8,128)(2,1)S(1)} %fusion.12), channel_id=1, source_target_pairs={{16,0},{32,16},{48,32},{64,48},{80,64},{96,80},{112,96},{128,112},... | collective-permute-start | bytes 3932168 | tf_op jit(solution)/shard_map/ppermute | solution.py:24
  192.7 2.6 %copy-start.13 = (bf16[3,640,640]{2,1,0:T(8,128)(2,1)S(1)}, bf16[3,640,640]{2,1,0:T(8,128)(2,1)}, u32[]{:S(2)}) copy-start(bf16[3,640,640]{2,1,0:T(8,128)(2,1)} %all-gather.7.cloned.1.call-done) | copy-start | bytes 7372804
  209.6 1.1 copy-start.3
  238.1 4.6 %copy-start.4 = (bf16[32,20480]{1,0:T(8,128)(2,1)S(1)}, bf16[32,20480]{1,0:T(8,128)(2,1)}, u32[]{:S(2)}) copy-start(bf16[32,20480]{1,0:T(8,128)(2,1)} %copy-done.3) | copy-start | bytes 3932164
  242.7 3.9 %copy-start.1 = (bf16[1,640,640]{2,1,0:T(8,128)(2,1)S(1)}, bf16[1,640,640]{2,1,0:T(8,128)(2,1)}, u32[]{:S(2)}) copy-start(bf16[1,640,640]{2,1,0:T(8,128)(2,1)} %param.14) | copy-start | bytes 2457604
Sparse Core Ops, SparseCore 0:
  9.8 71.1 all-gather.8
  82.7 51.3 all-gather.4
  135.9 38.4 all-gather.6
where the time goes:
time: 254 us; the launch traced here: 253 us
  waiting for transfers between devices  125 us (49%)
  matrix products  60.7 us (24%)
  local copies, waits for them, and re-layouts  19.9 us (8%)
  blocking collectives  18.4 us (7%)
  between operations  14.2 us (6%)
  starting transfers between devices  11.4 us (4%)
  other arithmetic  3.74 us (1%)
    all_gather x1, waiting for transfers between devices, per_device(): mine = lax.all_gather(own_half, BATCH, axis=0, tiled=False)  62.9 us
    all_gather x2, waiting for transfers between devices, gather_out_major(): return lax.all_gather(turned, FSDP, axis=1, tiled=True)  52.4 us
    dot_general x12, matrix products, nt_dot(): lax.dot_general(a, b, (((1,), (1,)), ((), ())), preferred_element_type=jn...  34 us
    all_gather x1, blocking collectives, per_device(): heads = lax.all_gather(critic_head[0], BATCH, axis=0, tiled=False)  18.4 us
    dot_general x1, matrix products, per_device(): jnp.einsum('gth,gch->gtc', slope_of(other, heads_other), other, preferred...  11.3 us
    dot_general x1, matrix products, per_device(): jnp.einsum('gth,gch->gtc', slope_of(mine, heads_mine), mine, preferred_el...  10.6 us
    ppermute x1, starting transfers between devices, with_halo(): after = lax.ppermute(leading, axis, down)  8.55 us
    ppermute x1, waiting for transfers between devices, with_halo(): after = lax.ppermute(leading, axis, down)  8.15 us
  transfers between devices with their start and end apart: 6, of which 3 were waited for; matrix products, arithmetic and copies ran while one was open for 24% of the time, Pallas kernels for 0%

commit v1 on v0

--- a/solution.py
+++ b/solution.py
@@ -12,6 +12,12 @@
 CAP = 4
 FSDP = ("z", "c")
 BATCH = ("y", "x")
+
+
+def unite_columns(matrix, where_dim, device_axis):
+    a_next = jnp.stack([matrix for _ in range(lax.axis_size(device_axis))])
+    new = lax.all_to_all(a_next, device_axis, 0, 0)
+    return jnp.concatenate(new, where_dim)
 
 
 def with_halo(array, axis, dim):
@@ -37,7 +43,7 @@
 
 def gather_out_major(weights):
     turned = jnp.swapaxes(weights, 1, 2)
-    return lax.all_gather(turned, FSDP, axis=1, tiled=True)
+    return unite_columns(turned, 1, FSDP)
 
 
 def nt_dot(a, b):

time: 254 us -> 309 us (1.22)
  waiting for transfers between devices: 125 us -> 165 us
  local copies, waits for them, and re-layouts: 19.9 us -> 32 us
  starting transfers between devices: 11.4 us -> 21.9 us
  matrix products: 60.7 us -> 50.3 us
    all_to_all x0 -> x2, waiting for transfers between devices: none -> 117 us  [unite_columns(): new = lax.all_to_all(a_next, device_axis, 0, 0)]
    all_gather x2 -> x0, waiting for transfers between devices: 52.4 us -> none  [gather_out_major(): return lax.all_gather(turned, FSDP, axis=1, tiled=True)]
    all_gather x1, waiting for transfers between devices: 62.9 us -> 41.1 us  [per_device(): mine = lax.all_gather(own_half, BATCH, axis=0, tiled=False)]
    all_to_all x0 -> x2, starting transfers between devices: none -> 15.5 us  [unite_columns(): new = lax.all_to_all(a_next, device_axis, 0, 0)]
    dot_general x12, matrix products: 34 us -> 23.5 us  [nt_dot(): lax.dot_general(a, b, (((1,), (1,)), ((), ())), preferred_element_type=jn...]
    ppermute x1, waiting for transfers between devices: 8.15 us -> 0.01 us  [with_halo(): after = lax.ppermute(leading, axis, down)]
    ppermute x1, waiting for transfers between devices: 0.01 us -> 6.69 us  [with_halo(): before = lax.ppermute(last, axis, up)]
    ppermute x1, starting transfers between devices: 8.55 us -> 1.93 us  [with_halo(): after = lax.ppermute(leading, axis, down)]
  transfers between devices with their start and end apart: 6 -> 6, of which waited for: 3 -> 4; matrix products, arithmetic and copies ran while one was open for 24% -> 20% of each run, Pallas kernels for 0% -> 0%
where the time goes in v1:
time: 309 us; the launch traced here: 308 us
  waiting for transfers between devices  165 us (53%)
  matrix products  50.3 us (16%)
  local copies, waits for them, and re-layouts  32 us (10%)
  starting transfers between devices  21.9 us (7%)
  blocking collectives  20.7 us (7%)
  between operations  14.5 us (5%)
  other arithmetic  4.57 us (1%)
    all_to_all x2, waiting for transfers between devices, unite_columns(): new = lax.all_to_all(a_next, device_axis, 0, 0)  117 us
    all_gather x1, waiting for transfers between devices, per_device(): mine = lax.all_gather(own_half, BATCH, axis=0, tiled=False)  41.1 us
    dot_general x12, matrix products, nt_dot(): lax.dot_general(a, b, (((1,), (1,)), ((), ())), preferred_element_type=jn...  23.5 us
    all_gather x1, blocking collectives, per_device(): heads = lax.all_gather(critic_head[0], BATCH, axis=0, tiled=False)  20.7 us
    all_to_all x2, starting transfers between devices, unite_columns(): new = lax.all_to_all(a_next, device_axis, 0, 0)  15.5 us
    dot_general x1, matrix products, per_device(): jnp.einsum('gth,gch->gtc', slope_of(other, heads_other), other, preferred...  11.5 us
    dot_general x1, matrix products, per_device(): jnp.einsum('gth,gch->gtc', slope_of(mine, heads_mine), mine, preferred_el...  10.6 us
    ppermute x1, waiting for transfers between devices, with_halo(): before = lax.ppermute(last, axis, up)  6.69 us
  transfers between devices with their start and end apart: 6, of which 4 were waited for; matrix products, arithmetic and copies ran while one was open for 20% of the time, Pallas kernels for 0%

profile of v1, /device:TPU:1, one launch (start us, length us, event | category | flops | bytes accessed | tf_op | source)
XLA Modules:
  0.0 308.4 jit_solution(11979884880462471557)
XLA Ops:
  6.5 4.7 %stack.4 = bf16[16,9,40,640]{3,2,1,0:T(8,128)(2,1)} broadcast(bf16[9,40,640]{2,1,0:T(8,128)(2,1)} %bitcast.102), dimensions={1,2,3} | broadcast | bytes 7833600 | tf_op jit(solution)/shard_map/stack | solution.py:18
  11.2 10.0 %all-to-all-start = ((bf16[16,9,40,640]{3,2,1,0:T(8,128)(2,1)}), bf16[16,9,40,640]{3,2,1,0:T(8,128)(2,1)}, u32[]{:S(2)}, u32[]{:S(2)}) async-start(bf16[16,9,40,640]{3,2,1,0:T(8,128)(2,1)} %stack.4), calls=%async_computation | async-start | bytes 14745600 | tf_op jit(solution)/shard_map/all_to_all | solution.py:19
  24.8 20.7 %all-gather = f32[16,1,640]{2,1,0:T(1,128)S(1)} all-gather(f32[1,1,640]{2,1,0:T(1,128)S(1)} %bitcast.104), channel_id=1, replica_groups=mesh['z'=8,'c'=2,'y'=4,'x'=4] {'y','x'}, dimensions={0}, use_global_device_ids=true | all-gather | bytes 43520 | tf_op jit(solution)/shard_map/all_gather | solution.py:64
  46.3 5.3 %pad_slice_fusion = (bf16[1,32,32,640]{3,2,1,0:T(8,128)(2,1)}, bf16[1,32,32,640]{3,2,1,0:T(8,128)(2,1)}, bf16[1,32,32,640]{3,2,1,0:T(8,128)(2,1)}, bf16[1,32,32,...) fusion(bf16[1,32,32,640]{3,2,1,0:T(8,128)(2,1)S(1)} %bitcast.81), kind=kLoop, calls=%fused_computation.34 | loop fusion | bytes 11796480 | tf_op jit(solution)/shard_map/slice | solution.py:76
  51.6 41.1 %all-gather.3.cloned.1.call-done = bf16[16,640,320]{1,2,0:T(8,128)(2,1)} async-done(((bf16[1,640,320]{1,2,0:T(8,128)(2,1)}), bf16[16,640,320]{1,2,0:T(8,128)(2,1)}) %all-gather.3.cloned.1.call-update) | async-done | bytes 6553616 | tf_op jit(solution)/shard_map/all_gather | solution.py:62
  93.6 89.2 %all-to-all-done = bf16[16,9,40,640]{3,2,1,0:T(8,128)(2,1)} async-done(((bf16[16,9,40,640]{3,2,1,0:T(8,128)(2,1)}), bf16[16,9,40,640]{3,2,1,0:T(8,128)(2,1)}, u32[]{:S(2)}, u32[]{:S(2)}) %all-to-all-start) | async-done | bytes 7372832 | tf_op jit(solution)/shard_map/all_to_all | solution.py:19
  182.8 1.6 stack.5
  184.4 5.6 %all-to-all-start.1 = ((bf16[16,3,40,640]{3,2,1,0:T(8,128)(2,1)}), bf16[16,3,40,640]{3,2,1,0:T(8,128)(2,1)}, u32[]{:S(2)}, u32[]{:S(2)}) async-start(bf16[16,3,40,640]{3,2,1,0:T(8,128)(2,1)} %stack.5), calls=%async_computation.1 | async-start | bytes 4915200 | tf_op jit(solution)/shard_map/all_to_all | solution.py:19
  190.0 3.9 %fusion.46 = (bf16[1,16,40,640]{3,2,0,1:T(8,128)(2,1)S(1)}, bf16[1,16,40,640]{3,2,0,1:T(8,128)(2,1)S(1)}, bf16[1,16,40,640]{3,2,0,1:T(8,128)(2,1)S(1)}, bf16[1,1...) fusion(bf16[9,16,40,640]{3,2,0,1:T(8,128)(2,1)} %bitcast.3), kind=kLoop, calls=%fused_computation.74 | loop fusion | bytes 14745600 | tf_op jit(solution)/shard_map/slice | solution.py:79
  196.6 1.3 fusion.49
  198.0 1.3 fusion.50
  199.3 1.3 fusion.51
  202.0 1.3 fusion.53
  203.4 2.8 fusion.54
  206.2 3.5 %convert_reduce_fusion = (f32[640]{0:T(1024)S(1)}, bf16[1,1,1024,640]{3,2,1,0:T(8,128)(2,1)S(1)}) fusion(bf16[1024,640]{1,0:T(8,128)(2,1)S(1)} %bitcast.82, bf16[640,640]{1,0:T(8,128)(2,1)S(1)} %bitcast.84, f32[1024,640]{1,0:T(8,128)} %fusion.54, f32[1024,640]{1,0:T(8,128)S(1)} %fusion.53, f32[1024,640]{1,0:T(8,128)S(1)} %fusion.52, ...), kind=kOutput, calls=%fused_computation.6 | convolution fusion | flops 847379840 | bytes 25725440 | tf_op jit(solution)/shard_map/dot_general | solution.py:50
  211.1 1.9 fusion.12
  213.0 3.5 %collective-permute-start = (bf16[1,1,1024,640]{3,2,1,0:T(8,128)(2,1)}, bf16[1,1,1024,640]{3,2,1,0:T(8,128)(2,1)}, u32[]{:S(2)}, u32[]{:S(2)}) collective-permute-start(bf16[1,1,1024,640]{3,2,1,0:T(8,128)(2,1)} %fusion.12), channel_id=1, source_target_pairs={{0,16},{16,32},{32,48},{48,64},{64,80},{80,96},{96,112},{112,128},... | collective-permute-start | bytes 3932168 | tf_op jit(solution)/shard_map/ppermute | solution.py:29
  216.8 1.9 collective-permute-start.1
  218.9 27.5 %all-to-all-done.1 = bf16[16,3,40,640]{3,2,1,0:T(8,128)(2,1)} async-done(((bf16[16,3,40,640]{3,2,1,0:T(8,128)(2,1)}), bf16[16,3,40,640]{3,2,1,0:T(8,128)(2,1)}, u32[]{:S(2)}, u32[]{:S(2)}) %all-to-all-start.1) | async-done | bytes 2457632 | tf_op jit(solution)/shard_map/all_to_all | solution.py:19
  246.4 1.9 fusion.47
  248.2 2.6 fusion.28
  250.9 6.7 %collective-permute-done = bf16[1,1,1024,640]{3,2,1,0:T(8,128)(2,1)} collective-permute-done((bf16[1,1,1024,640]{3,2,1,0:T(8,128)(2,1)}, bf16[1,1,1024,640]{3,2,1,0:T(8,128)(2,1)}, u32[]{:S(2)}, u32[]{:S(2)}) %collective-permute-start) | collective-permute-done | bytes 1310752 | tf_op jit(solution)/shard_map/ppermute | solution.py:29
  257.6 2.6 fusion.30
  260.2 2.6 fusion.22
  262.8 1.7 reshape.255
  265.6 2.3 convolution_convert_fusion
  267.9 3.1 %reshape.257 = bf16[16,128,640]{2,1,0:T(8,128)(2,1)S(1)} reshape(bf16[64,20480]{1,0:T(8,128)(2,1)} %convolution_convert_fusion) | data formatting | bytes 5242880 | tf_op jit(solution)/shard_map/reshape | solution.py:104
  271.1 10.6 %fusion.23 = f32[16,128,640]{2,1,0:T(8,128)} fusion(bf16[16,640,320]{1,2,0:T(8,128)(2,1)} %all-gather.3.cloned.1.call-done, bf16[16,128,640]{2,1,0:T(8,128)(2,1)S(1)} %reshape.257, f32[16,320]{1,0:T(8,128)S(1)} %get-tuple-element.30), kind=kOutput, calls=%fused_computation.42 | convolution fusion | flops 1680343040 | bytes 14438400 | tf_op jit(solution)/shard_map/gth,gch->gtc/dot_general | solution.py:111
  281.6 11.5 %add_convert_fusion = bf16[16,128,640]{2,1,0:T(8,128)(2,1)} fusion(f32[16,128,640]{2,1,0:T(8,128)} %fusion.23, bf16[16,640,320]{1,2,0:T(8,128)(2,1)} %collective-permute-done.2, bf16[16,128,640]{2,1,0:T(8,128)(2,1)S(1)} %reshape.257, f32[16,320]{1,0:T(8,128)S(1)} %get-tuple-element.29), kind=kOutput, calls=%fused_computation.3 | convolution fusion | flops 1682964480 | bytes 17059840 | tf_op jit(solution)/shard_map/gth,gch->gtc/dot_general | solution.py:113
  293.1 4.6 %reshape.258 = bf16[64,20480]{1,0:T(8,128)(2,1)} reshape(bf16[16,128,640]{2,1,0:T(8,128)(2,1)} %add_convert_fusion) | data formatting | bytes 5242880 | tf_op jit(solution)/shard_map/reshape | solution.py:116
  297.7 2.4 fusion
  300.1 1.5 reshape.259
  (76 shorter events, 11.3 us)
Async XLA Ops:
  6.5 14.7 %copy-start = (bf16[1,640,640]{2,1,0:T(8,128)(2,1)S(1)}, bf16[1,640,640]{2,1,0:T(8,128)(2,1)}, u32[]{:S(2)}) copy-start(bf16[1,640,640]{2,1,0:T(8,128)(2,1)} %param.14) | copy-start | bytes 2457604
  11.2 171.6 %all-to-all-start = ((bf16[16,9,40,640]{3,2,1,0:T(8,128)(2,1)}), bf16[16,9,40,640]{3,2,1,0:T(8,128)(2,1)}, u32[]{:S(2)}, u32[]{:S(2)}) async-start(bf16[16,9,40,640]{3,2,1,0:T(8,128)(2,1)} %stack.4), calls=%async_computation | async-start | bytes 14745600 | tf_op jit(solution)/shard_map/all_to_all | solution.py:19
  21.2 1.3 copy-start.2
  21.2 2.8 copy-start.17
  21.2 3.6 %copy-start.16 = (f32[1,640]{1,0:T(1,128)S(1)}, f32[1,640]{1,0:T(1,128)}, u32[]{:S(2)}) copy-start(f32[1,640]{1,0:T(1,128)} %param.15) | copy-start | bytes 7684
  21.2 24.3 %copy-start.14 = (f32[640]{0:T(1024)S(1)}, f32[640]{0:T(1024)}, u32[]{:S(2)}) copy-start(f32[640]{0:T(1024)} %param.10) | copy-start | bytes 7684
  21.2 71.5 %all-gather.3.cloned.1.call-start = ((), (), s32[]{:S(2)}) async-start(), calls=%async_computation.2 | async-start | bytes 6963200 | tf_op jit(solution)/shard_map/all_gather | solution.py:62
  46.3 136.5 %copy-start.13 = (bf16[3,640,40]{1,2,0:T(8,128)(2,1)S(1)}, bf16[3,640,40]{1,2,0:T(8,128)(2,1)}, u32[]{:S(2)}) copy-start(bf16[3,640,40]{1,2,0:T(8,128)(2,1)} %param.13) | copy-start | bytes 460804
  92.7 188.9 %collective-permute-start.2 = (bf16[16,640,320]{1,2,0:T(8,128)(2,1)}, bf16[16,640,320]{1,2,0:T(8,128)(2,1)}, u32[]{:S(2)}, u32[]{:S(2)}) collective-permute-start(bf16[16,640,320]{1,2,0:T(8,128)(2,1)} %all-gather.3.cloned.1.call-done), channel_id=1, source_target_pairs={{0,16},{16,0},{1,17},{17,1},{2,18},{18,2},{3,19},{19,3},{4,20},{20... | collective-permute-start | bytes 19660808 | tf_op jit(solution)/shard_map/ppermute | solution.py:63
  184.4 62.0 %all-to-all-start.1 = ((bf16[16,3,40,640]{3,2,1,0:T(8,128)(2,1)}), bf16[16,3,40,640]{3,2,1,0:T(8,128)(2,1)}, u32[]{:S(2)}, u32[]{:S(2)}) async-start(bf16[16,3,40,640]{3,2,1,0:T(8,128)(2,1)} %stack.5), calls=%async_computation.1 | async-start | bytes 4915200 | tf_op jit(solution)/shard_map/all_to_all | solution.py:19
  193.9 1.4 copy-start.12
  195.2 1.4 copy-start.11
  196.6 1.4 copy-start.10
  198.0 1.4 copy-start.9
  199.3 1.4 copy-start.8
  200.7 1.4 copy-start.7
  202.0 1.4 copy-start.6
  203.4 2.9 copy-start.5
  206.2 4.9 %copy-start.15 = (f32[640]{0:T(1024)S(1)}, f32[640]{0:T(1024)}, u32[]{:S(2)}) copy-start(f32[640]{0:T(1024)} %param.11) | copy-start | bytes 7684
  213.0 44.5 %collective-permute-start = (bf16[1,1,1024,640]{3,2,1,0:T(8,128)(2,1)}, bf16[1,1,1024,640]{3,2,1,0:T(8,128)(2,1)}, u32[]{:S(2)}, u32[]{:S(2)}) collective-permute-start(bf16[1,1,1024,640]{3,2,1,0:T(8,128)(2,1)} %fusion.12), channel_id=1, source_target_pairs={{0,16},{16,32},{32,48},{48,64},{64,80},{80,96},{96,112},{112,128},... | collective-permute-start | bytes 3932168 | tf_op jit(solution)/shard_map/ppermute | solution.py:29
  216.8 43.5 %collective-permute-start.1 = (bf16[1,1,1024,640]{3,2,1,0:T(8,128)(2,1)}, bf16[1,1,1024,640]{3,2,1,0:T(8,128)(2,1)S(1)}, u32[]{:S(2)}, u32[]{:S(2)}) collective-permute-start(bf16[1,1,1024,640]{3,2,1,0:T(8,128)(2,1)} %fusion.12), channel_id=1, source_target_pairs={{16,0},{32,16},{48,32},{64,48},{80,64},{96,80},{112,96},{128,112},... | collective-permute-start | bytes 3932168 | tf_op jit(solution)/shard_map/ppermute | solution.py:30
  264.5 1.1 copy-start.3
  293.1 4.6 %copy-start.4 = (bf16[32,20480]{1,0:T(8,128)(2,1)S(1)}, bf16[32,20480]{1,0:T(8,128)(2,1)}, u32[]{:S(2)}) copy-start(bf16[32,20480]{1,0:T(8,128)(2,1)} %copy-done.3) | copy-start | bytes 3932164
  297.7 3.9 %copy-start.1 = (bf16[1,640,640]{2,1,0:T(8,128)(2,1)S(1)}, bf16[1,640,640]{2,1,0:T(8,128)(2,1)}, u32[]{:S(2)}) copy-start(bf16[1,640,640]{2,1,0:T(8,128)(2,1)} %param.14) | copy-start | bytes 2457604
Sparse Core Ops, SparseCore 0:
  24.5 68.2 all-gather.2
